TPU v7x, 128 devices: a whole 4x4x4 slice. The times are simulated.
128 devices in a mesh: ens: 8 (over y, core), trc: 16 (over z, x).
Axes of the slice: x: 4, y: 4, z: 4, core: 2. Of those that a mesh axis runs over, the one named last changes fastest.
Arguments:
- tracer_state: bfloat16 [3072, 4, 16, 1440], P(('ens', 'trc')), may hold values from -6 to 6
- velocity: float32 [2, 4, 16, 1440], replicated, may hold values from -0.24 to 0.24
- land_mask: int32 [16, 1440], replicated, may hold values from 0 to 1, as said below
- in_weight: bfloat16 [24, 256], replicated, may hold values from -1.25 to 1.25
- bias_one: float32 [256], replicated, may hold values from -3 to 3
- hid_weight: bfloat16 [256, 256], replicated, may hold values from -0.375 to 0.375
- bias_two: float32 [256], replicated, may hold values from -3 to 3
- out_coef: float32 [128, 24, 256], P('ens'), may hold values from -6 to 6
- obs_cell: int32 [16, 128], P('trc'), may hold values from 0 to 5759, as said below
- obs_count: int32 [16], P('trc'), may hold values from 16 to 128, as said below
- obs_value: float32 [16, 6, 128], P('trc'), may hold values from -6 to 6
- obs_var: float32 [16, 6, 128], P('trc'), may hold values from 0.05 to 0.5
- obs_noise: float32 [128, 16, 6, 128], P(None, 'trc'), may hold values from -2 to 2
Outputs:
- new_state: bfloat16 [3072, 4, 16, 1440], P('ens', None, 'trc')
- new_coef: float32 [128, 24, 256], P('ens')
Inputs may be any that keep to these rules, and one draw needn't show every extreme that they name: `land_mask`: every block of 1 latitude rows (rows k * 1 to (k + 1) - 1) holds at most 1152 ocean columns, and some block exactly 1152. `obs_cell`: every slot names an ocean cell of its block. `obs_count`: some block uses all 128 slots.
All inputs are finite; a program needn't handle non-finite values.
Results may differ from a plain program's by a relative error of at most 0.0068.
Values may be sent and summed in bfloat16 or wider, within the bound.
No kernel may reach another device: no remote copies, remote signals or barrier semaphores. Data moves between devices by JAX's collectives and lax.ppermute only.
A program may use at most 128 MiB of HBM per device.

v0:
```python
import jax
import jax.numpy as jnp
from jax import lax
from jax.sharding import PartitionSpec as P

OBS_TR = 6
ADV_STEPS = 2
OBS_CAP = 128


def transport(concentration, velocity, sea_mask):
    east_open = sea_mask * jnp.roll(sea_mask, -1, axis=1)
    north_open = sea_mask * jnp.concatenate([sea_mask[1:], jnp.zeros_like(sea_mask[:1])], axis=0)
    east_speed = velocity[0] * east_open
    north_speed = velocity[1] * north_open
    for _ in range(ADV_STEPS):
        east_value = jnp.roll(concentration, -1, axis=-1)
        east_flux = (
            jnp.maximum(east_speed, 0.0) * concentration + jnp.minimum(east_speed, 0.0) * east_value
        )
        north_value = jnp.concatenate(
            [concentration[..., 1:, :], jnp.zeros_like(concentration[..., :1, :])], axis=-2
        )
        north_flux = (
            jnp.maximum(north_speed, 0.0) * concentration
            + jnp.minimum(north_speed, 0.0) * north_value
        )
        west_flux = jnp.roll(east_flux, 1, axis=-1)
        south_flux = jnp.concatenate(
            [jnp.zeros_like(north_flux[..., :1, :]), north_flux[..., :-1, :]], axis=-2
        )
        concentration = concentration - (east_flux - west_flux) - (north_flux - south_flux)
    return concentration


def silu(value):
    return value * (0.5 + 0.5 * jnp.tanh(0.5 * value))


def tree_sum(value, axis_name, size):
    if size & size - 1:
        return lax.psum(value, axis_name)
    step = 1
    while step < size:
        pairs = [(i, i ^ step) for i in range(size)]
        value = value + lax.ppermute(value, axis_name, pairs)
        step *= 2
    return value


def reaction(fields, in_weight, bias_one, hid_weight, bias_two, member_coef, sea_cells):
    contract = (((0,), (0,)), ((), ()))
    hidden_one = lax.dot_general(in_weight, fields, contract, preferred_element_type=jnp.float32)
    hidden_one = silu(hidden_one + bias_one[:, None]).astype(jnp.bfloat16)
    hidden_two = lax.dot_general(
        hid_weight, hidden_one, contract, preferred_element_type=jnp.float32
    )
    hidden_two = silu(hidden_two + bias_two[:, None]).astype(jnp.bfloat16)
    tendency = jnp.dot(
        member_coef, hidden_two, preferred_element_type=jnp.float32
    ) * hid_weight.shape[0] ** (-0.5)
    return ((fields.astype(jnp.float32) + tendency) * sea_cells).astype(jnp.bfloat16)


def solve_system(system, right_side):
    factor = jnp.linalg.cholesky(system)
    middle = lax.linalg.triangular_solve(factor, right_side, left_side=True, lower=True)
    return lax.linalg.triangular_solve(factor, middle, left_side=True, lower=True, transpose_a=True)


def shards(
    tracer_state,
    velocity,
    land_mask,
    in_weight,
    bias_one,
    hid_weight,
    bias_two,
    out_coef,
    obs_cell,
    obs_count,
    obs_value,
    obs_var,
    obs_noise,
):
    blocks = lax.axis_size("trc")
    own_block = lax.axis_index("trc")
    group_index = lax.axis_index("ens")
    field_rows, levels, lat_rows, lon_count = tracer_state.shape
    row_block = lat_rows // blocks
    block_width = row_block * lon_count
    members_here = out_coef.shape[0]
    tracers = in_weight.shape[0]
    group_rows = members_here * tracers
    highest = lax.Precision.HIGHEST
    sea_mask = land_mask.astype(jnp.float32)
    coef_all = lax.all_gather(out_coef.reshape(out_coef.shape[0], -1), "ens", axis=0, tiled=True)
    advected = transport(tracer_state.astype(jnp.float32) * sea_mask, velocity, sea_mask).astype(
        jnp.bfloat16
    )
    coef_half = out_coef.astype(jnp.bfloat16)
    sea_own = lax.dynamic_slice_in_dim(sea_mask, own_block * row_block, row_block, 0)
    gathered = lax.all_to_all(advected, "trc", split_axis=2, concat_axis=0, tiled=True)
    out_shape = gathered.shape
    grouped = gathered.reshape(members_here, tracers, -1)
    sea_cells = jnp.broadcast_to(sea_own[None], (out_shape[1],) + sea_own.shape).reshape(-1)

    def one_member(inputs):
        fields, member_coef = inputs
        return reaction(fields, in_weight, bias_one, hid_weight, bias_two, member_coef, sea_cells)

    reacted = lax.map(one_member, (grouped, coef_half))
    new_cols = reacted.reshape(out_shape)
    new_flat = new_cols.reshape(group_rows, levels, block_width)
    observed = new_flat.reshape(members_here, tracers, levels * block_width)[:, :OBS_TR]
    observed = observed.reshape(members_here * OBS_TR, levels * block_width)
    cell_ids = lax.broadcasted_iota(jnp.int32, (levels * block_width, OBS_CAP), 0)
    picker = (cell_ids == obs_cell[0][None, :]).astype(jnp.bfloat16)
    picked = jnp.dot(observed, picker, preferred_element_type=jnp.float32)
    predicted_own = picked.astype(jnp.bfloat16).reshape(members_here, OBS_TR, OBS_CAP)
    predicted_all = lax.all_gather(predicted_own, "ens", axis=0, tiled=True)
    member_total = predicted_all.shape[0]
    slot_ids = jnp.arange(OBS_CAP, dtype=jnp.int32)
    valid_slots = (slot_ids < obs_count[0]).astype(jnp.float32)
    weight = valid_slots[None, :] / obs_var[0]
    guessed = predicted_all.astype(jnp.float32).reshape(member_total, -1)
    anomaly = guessed - jnp.mean(guessed, axis=0)
    misfit = (obs_value[None] + obs_noise).reshape(member_total, -1) - guessed
    weighted = anomaly * weight.reshape(1, -1)
    gram_part = jnp.dot(weighted, anomaly.T, precision=highest, preferred_element_type=jnp.float32)
    cross_part = jnp.dot(weighted, misfit.T, precision=highest, preferred_element_type=jnp.float32)
    both = tree_sum(jnp.stack([gram_part, cross_part]), "trc", blocks)
    gram, cross = (both[0], both[1])
    system = (member_total - 1) * jnp.eye(member_total, dtype=jnp.float32) + gram
    mixing = solve_system(system, cross)
    flat_coef = out_coef.reshape(members_here, -1)
    first_member = group_index * members_here
    mixing_cols = lax.dynamic_slice_in_dim(mixing, first_member, members_here, 1)
    summed = jnp.dot(mixing_cols.T, coef_all, precision=highest, preferred_element_type=jnp.float32)
    new_coef = flat_coef + summed
    return (new_cols, new_coef.reshape(members_here, tracers, -1))


def solution(mesh):
    in_specs = (
        P(("ens", "trc"), None, None, None),
        P(),
        P(),
        P(),
        P(),
        P(),
        P(),
        P("ens", None, None),
        P("trc", None),
        P("trc"),
        P("trc", None, None),
        P("trc", None, None),
        P(None, "trc", None, None),
    )
    out_specs = (P("ens", None, "trc", None), P("ens", None, None))
    return jax.shard_map(shards, mesh=mesh, in_specs=in_specs, out_specs=out_specs, check_vma=False)
```

profile of v0, /device:TPU:6, one launch (start us, length us, event | category | flops | bytes accessed | tf_op | source)
XLA Modules:
  0.0 444.6 jit_solution(4422173835736729489)
XLA Ops:
  8.2 5.3 %convert_multiply_fusion = f32[24,4,16,1440]{3,0,1,2:T(8,128)S(1)} fusion(f32[16,1440]{1,0:T(8,128)S(1)} %convert_element_type.40, bf16[24,4,16,1440]{3,2,1,0:T(8,128)(2,1)} %param.15), kind=kLoop, calls=%fused_computation.34 | loop fusion | flops 4423680 | bytes 13363200 | tf_op jit(solution)/shard_map/mul | solution.py:98
  13.4 6.1 %slice.102 = f32[24,4,16,1439]{3,0,1,2:T(8,128)} slice(f32[24,4,16,1440]{3,0,1,2:T(8,128)S(1)} %convert_multiply_fusion), slice={[0:24], [0:4], [0:16], [1:1440]} | slice | bytes 17682432 | tf_op jit(solution)/shard_map/jit(_roll_static)/slice | solution.py:17
  19.6 4.2 slice.107
  26.1 13.3 %multiply_add_fusion.1 = (f32[24,4,16,1440]{3,0,1,2:T(8,128)S(1)}, f32[24,4,16,1440]{3,0,1,2:T(8,128)S(1)}) fusion(f32[24,4,15,1440]{3,0,1,2:T(8,128)} %slice.107, f32[4,16,1440]{2,0,1:T(4,128)S(1)} %copy.69, f32[4,16,1440]{2,0,1:T(4,128)S(1)} %copy.68, f32[16,1440]{1,0:T(8,128)S(1)} %convert_element_type.40, bf16[24,4,16,1440]{3,2,1,0:T(8,128)(2,1)} %param.15, ...), kind=kLoop, calls=%fused_computation.33 | loop fusion | flops 19906560 | bytes 40826880 | tf_op jit(solution)/shard_map/add | solution.py:25
  39.4 4.8 %slice.108 = f32[24,4,15,1440]{3,0,1,2:T(8,128)} slice(f32[24,4,16,1440]{3,0,1,2:T(8,128)S(1)} %get-tuple-element.101), slice={[0:24], [0:4], [0:15], [0:1440]} | slice | bytes 16588800 | tf_op jit(solution)/shard_map/slice | solution.py:30
  44.2 2.4 slice.104
  46.6 2.1 copy-done.1
  48.7 15.4 %fusion.18 = f32[24,4,16,1440]{3,0,1,2:T(8,128)S(1)} fusion(f32[24,4,16,1440]{3,0,1,2:T(8,128)} %copy-done, f32[24,4,16,1439]{3,0,1,2:T(8,128)} %bitcast.104, f32[24,4,16,1]{3,0,1,2:T(8,128)} %slice.104, f32[24,4,16,1440]{3,0,1,2:T(8,128)} %copy-done.1, f32[24,4,15,1440]{3,0,1,2:T(8,128)} %slice.108, f32[16,1440]{1,0:T(8,128)S(1)} %convert_element_type.40, ...), kind=kLoop, calls=%fused_computation.25 | loop fusion | flops 15482880 | bytes 48199680 | tf_op jit(solution)/shard_map/sub | solution.py:32
  64.1 6.2 %slice.109 = f32[24,4,16,1439]{3,0,1,2:T(8,128)} slice(f32[24,4,16,1440]{3,0,1,2:T(8,128)S(1)} %fusion.18), slice={[0:24], [0:4], [0:16], [1:1440]} | slice | bytes 17682432 | tf_op jit(solution)/shard_map/jit(_roll_static)/slice | solution.py:17
  70.3 4.3 slice.113
  74.7 17.6 %multiply_add_fusion = (f32[24,4,16,1440]{3,0,1,2:T(8,128)}, f32[24,4,16,1440]{3,0,1,2:T(8,128)}) fusion(f32[24,4,15,1440]{3,0,1,2:T(8,128)} %slice.113, f32[24,4,16,1440]{3,0,1,2:T(8,128)S(1)} %fusion.18, f32[4,16,1440]{2,0,1:T(4,128)S(1)} %copy.69, f32[4,16,1440]{2,0,1:T(4,128)S(1)} %copy.68, f32[24,4,16,1]{3,0,1,2:T(8,128)S(1)} %slice.110, ...), kind=kLoop, calls=%fused_computation.32 | loop fusion | flops 15482880 | bytes 45158400 | tf_op jit(solution)/shard_map/add | solution.py:25
  92.3 8.2 %slice.114 = f32[24,4,15,1440]{3,0,1,2:T(8,128)} slice(f32[24,4,16,1440]{3,0,1,2:T(8,128)} %get-tuple-element.99), slice={[0:24], [0:4], [0:15], [0:1440]} | slice | bytes 16588800 | tf_op jit(solution)/shard_map/slice | solution.py:30
  100.5 1.4 slice.111
  101.9 16.1 %fusion.22 = bf16[24,4,16,1440]{3,0,1,2:T(8,128)(2,1)} fusion(f32[24,4,16,1440]{3,0,1,2:T(8,128)S(1)} %fusion.18, f32[24,4,16,1440]{3,0,1,2:T(8,128)} %get-tuple-element.100, f32[24,4,16,1439]{3,0,1,2:T(8,128)} %bitcast.103, f32[24,4,16,1]{3,0,1,2:T(8,128)S(1)} %slice.111, f32[24,4,16,1440]{3,0,1,2:T(8,128)} %get-tuple-element.99, f32[24,4,15,1440]{3,0,1,2:T(8,128)} %slice.114), kind=kLoop, calls=%fused_computation.31 | loop fusion | flops 13271040 | bytes 48107520 | tf_op jit(solution)/shard_map/convert_element_type | solution.py:98
  118.0 8.4 %all-to-all-start = ((bf16[24,4,16,1440]{3,0,1,2:T(8,128)(2,1)}), bf16[24,4,16,1440]{3,0,1,2:T(8,128)(2,1)}, u32[]{:S(2)}, u32[]{:S(2)}) async-start(bf16[24,4,16,1440]{3,0,1,2:T(8,128)(2,1)} %fusion.22), calls=%async_computation | async-start | bytes 9437184 | tf_op jit(solution)/shard_map/all_to_all | solution.py:103
  128.2 67.1 %all-to-all-done = bf16[24,4,16,1440]{3,0,1,2:T(8,128)(2,1)} async-done(((bf16[24,4,16,1440]{3,0,1,2:T(8,128)(2,1)}), bf16[24,4,16,1440]{3,0,1,2:T(8,128)(2,1)}, u32[]{:S(2)}, u32[]{:S(2)}) %all-to-all-start) | async-done | bytes 4423712 | tf_op jit(solution)/shard_map/all_to_all | solution.py:103
  195.3 7.0 %copy.70 = bf16[16,24,4,1,1440]{4,2,1,0,3:T(4,128)(2,1)} copy(bf16[16,24,4,1,1440]{4,1,2,0,3:T(8,128)(2,1)} %bitcast.5) | data formatting | bytes 8847360 | tf_op jit(solution)/shard_map/all_to_all | solution.py:103
  202.3 8.6 %reshape.103 = bf16[16,24,5760]{2,1,0:T(8,128)(2,1)} reshape(bf16[16,24,4,1,1440]{4,2,1,0,3:T(4,128)(2,1)} %copy.70) | data formatting | bytes 8847360 | tf_op jit(solution)/shard_map/reshape | solution.py:105
  210.9 138.9 %while.11 = (s32[]{:T(128)}, bf16[16,24,5760]{2,1,0:T(8,128)(2,1)}, bf16[16,24,5760]{2,1,0:T(8,128)(2,1)}, bf16[16,24,256]{2,1,0:T(8,128)(2,1)S(1)}, bf16[24,256...) while((s32[]{:T(128)}, bf16[16,24,5760]{2,1,0:T(8,128)(2,1)}, ...), condition=%wide.region_1.2_spmd.clone, body=%wide.region_0.1_spmd.clone.sunk | while | flops 914918400 | bytes 6986469 | solution.py:112
  210.9 4.2 multiply_convert_fusion.3
  215.3 4.4 fusion.59
  219.7 4.2 multiply_convert_fusion.3
  224.0 4.4 fusion.59
  228.4 4.2 multiply_convert_fusion.3
  232.7 4.4 fusion.59
  237.0 4.2 multiply_convert_fusion.3
  241.3 4.4 fusion.59
  245.7 4.2 multiply_convert_fusion.3
  250.0 4.4 fusion.59
  254.4 4.2 multiply_convert_fusion.3
  258.7 4.4 fusion.59
  263.1 4.2 multiply_convert_fusion.3
  267.4 4.4 fusion.59
  271.7 4.2 multiply_convert_fusion.3
  276.0 4.4 fusion.59
  280.4 4.2 multiply_convert_fusion.3
  284.7 4.4 fusion.59
  289.1 4.2 multiply_convert_fusion.3
  293.4 4.4 fusion.59
  297.8 4.2 multiply_convert_fusion.3
  302.1 4.4 fusion.59
  306.5 4.2 multiply_convert_fusion.3
  310.8 4.4 fusion.59
  315.1 4.2 multiply_convert_fusion.3
  319.4 4.4 fusion.59
  323.8 4.2 multiply_convert_fusion.3
  328.1 4.4 fusion.59
  332.5 4.2 multiply_convert_fusion.3
  336.8 4.4 fusion.59
  341.2 4.2 multiply_convert_fusion.3
  345.5 4.4 fusion.59
  349.8 1.5 slice.97
  352.6 13.5 %all_gather.6 = bf16[128,6,128]{2,0,1:T(8,128)(2,1)S(1)} all-gather(bf16[16,6,128]{2,0,1:T(8,128)(2,1)S(1)} %copy.71), channel_id=1, replica_groups=mesh['ens'=8,'trc'=16] {'ens'}, dimensions={0}, use_global_device_ids=true | all-gather | bytes 221184 | tf_op jit(solution)/shard_map/all_gather | solution.py:121
  367.9 1.2 convolution_bitcast_fusion.1
  369.2 5.7 %collective-permute-done = f32[2,128,128]{2,1,0:T(8,128)S(1)} collective-permute-done((f32[2,128,128]{2,1,0:T(8,128)S(1)}, f32[2,128,128]{2,1,0:T(8,128)S(1)}, u32[]{:S(2)}, u32[]{:S(2)}) %collective-permute-start) | collective-permute-done | bytes 131104 | tf_op jit(solution)/shard_map/ppermute | solution.py:46
  375.0 1.8 collective-permute-start.1
  376.8 4.7 %collective-permute-done.1 = f32[2,128,128]{2,1,0:T(8,128)S(1)} collective-permute-done((f32[2,128,128]{2,1,0:T(8,128)S(1)}, f32[2,128,128]{2,1,0:T(8,128)S(1)}, u32[]{:S(2)}, u32[]{:S(2)}) %collective-permute-start.1) | collective-permute-done | bytes 131104 | tf_op jit(solution)/shard_map/ppermute | solution.py:46
  382.1 4.5 %collective-permute-done.2 = f32[2,128,128]{2,1,0:T(8,128)S(1)} collective-permute-done((f32[2,128,128]{2,1,0:T(8,128)S(1)}, f32[2,128,128]{2,1,0:T(8,128)S(1)}, u32[]{:S(2)}, u32[]{:S(2)}) %collective-permute-start.2) | collective-permute-done | bytes 131104 | tf_op jit(solution)/shard_map/ppermute | solution.py:46
  386.6 3.6 collective-permute-start.3
  390.2 10.5 %reshape.104 = bf16[384,4,1,1440]{3,1,0,2:T(4,128)(2,1)} reshape(bf16[16,24,5760]{2,1,0:T(8,128)(2,1)} %get-tuple-element.49) | data formatting | bytes 8847360 | tf_op jit(solution)/shard_map/reshape | solution.py:113
  400.7 8.8 %copy.79 = bf16[384,4,1,1440]{0,3,2,1:T(8,128)(2,1)} copy(bf16[384,4,1,1440]{3,1,0,2:T(4,128)(2,1)} %reshape.104) | data formatting | bytes 8847360
  409.7 11.7 %cholesky.16 = f32[128,128]{1,0:T(8,128)S(1)} custom-call(f32[128,128]{1,0:T(8,128)S(1)} %fusion.35), custom_call_target="Cholesky" | custom-call | tf_op jit(solution)/shard_map/jit(cholesky)/cholesky | solution.py:66
  422.7 9.8 %custom-call.8 = f32[1,128,128]{1,2,0:T(8,128)S(1)} custom-call(f32[1,128,128]{2,1,0:T(8,128)S(1)} %fusion.29), custom_call_target="InvertDiagBlocksLowerTriangular" | custom-call | tf_op jit(solution)/shard_map/triangular_solve | solution.py:68
  433.1 3.5 convolution_add_fusion.2
  (110 shorter events, 13.0 us)
Async XLA Ops:
  19.6 5.2 %copy-start.6 = (s32[16,1440]{1,0:T(8,128)S(1)}, s32[16,1440]{1,0:T(8,128)}, u32[]{:S(2)}) copy-start(s32[16,1440]{1,0:T(8,128)} %param.17) | copy-start | bytes 276484
  19.6 5.3 %copy-start.4 = (f32[2,4,16,1440]{3,2,1,0:T(8,128)S(1)}, f32[2,4,16,1440]{3,2,1,0:T(8,128)}, u32[]{:S(2)}) copy-start(f32[2,4,16,1440]{3,2,1,0:T(8,128)} %param.16) | copy-start | bytes 2211844
  39.4 7.2 %copy-start = (f32[24,4,16,1440]{3,0,1,2:T(8,128)}, f32[24,4,16,1440]{3,0,1,2:T(8,128)S(1)}, u32[]{:S(2)}) copy-start(f32[24,4,16,1440]{3,0,1,2:T(8,128)S(1)} %get-tuple-element.102) | copy-start | bytes 26542084
  39.4 9.3 %copy-start.1 = (f32[24,4,16,1440]{3,0,1,2:T(8,128)}, f32[24,4,16,1440]{3,0,1,2:T(8,128)S(1)}, u32[]{:S(2)}) copy-start(f32[24,4,16,1440]{3,0,1,2:T(8,128)S(1)} %get-tuple-element.101) | copy-start | bytes 26542084
  118.0 8.5 %copy-start.3 = (f32[16,24,256]{2,1,0:T(8,128)S(1)}, f32[16,24,256]{2,1,0:T(8,128)}, u32[]{:S(2)}) copy-start(f32[16,24,256]{2,1,0:T(8,128)} %param.22) | copy-start | bytes 1179652
  118.0 10.2 %copy-start.7 = (f32[1,6,128]{2,0,1:T(1,128)S(1)}, f32[1,6,128]{2,0,1:T(1,128)}, u32[]{:S(2)}) copy-start(f32[1,6,128]{2,0,1:T(1,128)} %param.25) | copy-start | bytes 9220
  118.0 10.2 %copy-start.8 = (f32[1,6,128]{2,0,1:T(1,128)S(1)}, f32[1,6,128]{2,0,1:T(1,128)}, u32[]{:S(2)}) copy-start(f32[1,6,128]{2,0,1:T(1,128)} %param.26) | copy-start | bytes 9220
  118.0 77.3 %all-to-all-start = ((bf16[24,4,16,1440]{3,0,1,2:T(8,128)(2,1)}), bf16[24,4,16,1440]{3,0,1,2:T(8,128)(2,1)}, u32[]{:S(2)}, u32[]{:S(2)}) async-start(bf16[24,4,16,1440]{3,0,1,2:T(8,128)(2,1)} %fusion.22), calls=%async_computation | async-start | bytes 9437184 | tf_op jit(solution)/shard_map/all_to_all | solution.py:103
  126.4 306.7 %all-gather.2.cloned.1.call-start = ((), (), s32[]{:S(2)}) async-start(), calls=%async_computation.1 | async-start | bytes 3538944 | tf_op jit(solution)/shard_map/all_gather | solution.py:97
  127.4 83.5 %copy-start.9 = (bf16[256,256]{1,0:T(8,128)(2,1)S(1)}, bf16[256,256]{1,0:T(8,128)(2,1)}, u32[]{:S(2)}) copy-start(bf16[256,256]{1,0:T(8,128)(2,1)} %param.20) | copy-start | bytes 393220
  127.4 83.5 %copy-start.10 = (bf16[24,256]{1,0:T(8,128)(2,1)S(1)}, bf16[24,256]{1,0:T(8,128)(2,1)}, u32[]{:S(2)}) copy-start(bf16[24,256]{1,0:T(8,128)(2,1)} %param.18) | copy-start | bytes 36868
  127.4 83.5 %copy-start.11 = (f32[256]{0:T(256)S(1)}, f32[256]{0:T(256)}, u32[]{:S(2)}) copy-start(f32[256]{0:T(256)} %param.19) | copy-start | bytes 3076
  127.4 83.5 %copy-start.12 = (f32[256]{0:T(256)S(1)}, f32[256]{0:T(256)}, u32[]{:S(2)}) copy-start(f32[256]{0:T(256)} %param.21) | copy-start | bytes 3076
  210.9 140.9 %copy-start.13 = (s32[1,128]{1,0:T(1,128)S(1)}, s32[1,128]{1,0:T(1,128)}, u32[]{:S(2)}) copy-start(s32[1,128]{1,0:T(1,128)} %param.23) | copy-start | bytes 1540
  210.9 155.5 %copy-start.5 = (f32[128,1,6,128]{3,1,2,0:T(1,128)S(1)}, f32[128,1,6,128]{3,1,2,0:T(1,128)}, u32[]{:S(2)}) copy-start(f32[128,1,6,128]{3,1,2,0:T(1,128)} %param.27) | copy-start | bytes 1179652
  369.1 5.8 %collective-permute-start = (f32[2,128,128]{2,1,0:T(8,128)S(1)}, f32[2,128,128]{2,1,0:T(8,128)S(1)}, u32[]{:S(2)}, u32[]{:S(2)}) collective-permute-start(f32[2,128,128]{2,1,0:T(8,128)S(1)} %pad_maximum_fusion), channel_id=1, source_target_pairs={{0,1},{1,0},{2,3},{3,2},{4,5},{5,4},{6,7},{7,6},{8,9},{9,8},{10,11... | collective-permute-start | bytes 393224 | tf_op jit(solution)/shard_map/ppermute | solution.py:46
  375.0 6.6 %collective-permute-start.1 = (f32[2,128,128]{2,1,0:T(8,128)S(1)}, f32[2,128,128]{2,1,0:T(8,128)S(1)}, u32[]{:S(2)}, u32[]{:S(2)}) collective-permute-start(f32[2,128,128]{2,1,0:T(8,128)S(1)} %fusion.38), channel_id=1, source_target_pairs={{0,2},{1,3},{2,0},{3,1},{4,6},{5,7},{6,4},{7,5},{8,10},{9,11},{10,... | collective-permute-start | bytes 393224 | tf_op jit(solution)/shard_map/ppermute | solution.py:46
  381.5 5.0 %collective-permute-start.2 = (f32[2,128,128]{2,1,0:T(8,128)S(1)}, f32[2,128,128]{2,1,0:T(8,128)S(1)}, u32[]{:S(2)}, u32[]{:S(2)}) collective-permute-start(f32[2,128,128]{2,1,0:T(8,128)S(1)} %fusion.47), channel_id=1, source_target_pairs={{0,4},{1,5},{2,6},{3,7},{4,0},{5,1},{6,2},{7,3},{8,12},{9,13},{10,... | collective-permute-start | bytes 393224 | tf_op jit(solution)/shard_map/ppermute | solution.py:46
  386.6 22.9 %collective-permute-start.3 = (f32[2,128,128]{2,1,0:T(8,128)S(1)}, f32[2,128,128]{2,1,0:T(8,128)S(1)}, u32[]{:S(2)}, u32[]{:S(2)}) collective-permute-start(f32[2,128,128]{2,1,0:T(8,128)S(1)} %add.113), channel_id=1, source_target_pairs={{0,8},{1,9},{2,10},{3,11},{4,12},{5,13},{6,14},{7,15},{8,0},{9,1},... | collective-permute-start | bytes 393224 | tf_op jit(solution)/shard_map/ppermute | solution.py:46
  390.2 42.9 %copy-start.2 = (f32[2,8,24,256]{3,1,2,0:T(8,128)S(1)}, f32[2,8,24,256]{3,1,2,0:T(8,128)}, u32[]{:S(2)}) copy-start(f32[2,8,24,256]{3,1,2,0:T(8,128)} %copy.84) | copy-start | bytes 1179652
Sparse Core Ops, SparseCore 0:
  129.4 28.9 all-gather.1
where the time goes:
time: 452 us; the launch traced here: 445 us
  matrix products  144 us (32%)
  other arithmetic  92.1 us (20%)
  local copies, waits for them, and re-layouts  83.2 us (18%)
  waiting for transfers between devices  82.1 us (18%)
  between operations  15.4 us (3%)
  starting transfers between devices  14.5 us (3%)
  blocking collectives  13.5 us (3%)
    dot_general x16, matrix products, reaction(): jnp.dot(member_coef, hidden_two, preferred_element_type=jnp.float32)  70 us
    all_to_all x1, waiting for transfers between devices, shards(): lax.all_to_all(advected, 'trc', split_axis=2, concat_axis=0, tiled=True)  67.1 us
    dot_general x16, matrix products, reaction(): lax.dot_general(in_weight, fields, contract, preferred_element_type=jnp.f...  66.8 us
    add x2, other arithmetic, transport(): jnp.maximum(north_speed, 0.0) * concentration  30.8 us
    convert_element_type x1, other arithmetic, shards(): transport(tracer_state.astype(jnp.float32) * sea_mask, velocity, sea_mask)  16.1 us
    sub x1, other arithmetic, transport(): concentration - (east_flux - west_flux) - (north_flux - south_flux)  15.4 us
    ppermute x4, waiting for transfers between devices, tree_sum(): value = value + lax.ppermute(value, axis_name, pairs)  15 us
    all_gather x1, blocking collectives, shards(): predicted_all = lax.all_gather(predicted_own, 'ens', axis=0, tiled=True)  13.5 us
  transfers between devices with their start and end apart: 6, of which 4 were waited for; matrix products, arithmetic and copies ran while one was open for 46% of the time, Pallas kernels for 0%

commit v1 on v0

--- a/solution.py
+++ b/solution.py
@@ -2,10 +2,21 @@
 import jax.numpy as jnp
 from jax import lax
 from jax.sharding import PartitionSpec as P
+from jax.lax import all_to_all, axis_size
 
 OBS_TR = 6
 ADV_STEPS = 2
 OBS_CAP = 128
+
+
+def serve_the_rates(unit):
+    chip_axis = "ens"
+    world_n = axis_size(chip_axis)
+    log = []
+    for w in range(unit.ndim):
+        log.append(world_n if w == 0 else 1)
+    spare = jnp.tile(unit, log)
+    return all_to_all(spare, chip_axis, split_axis=0, concat_axis=0, tiled=True)
 
 
 def transport(concentration, velocity, sea_mask):
@@ -118,7 +129,7 @@
     picker = (cell_ids == obs_cell[0][None, :]).astype(jnp.bfloat16)
     picked = jnp.dot(observed, picker, preferred_element_type=jnp.float32)
     predicted_own = picked.astype(jnp.bfloat16).reshape(members_here, OBS_TR, OBS_CAP)
-    predicted_all = lax.all_gather(predicted_own, "ens", axis=0, tiled=True)
+    predicted_all = serve_the_rates(predicted_own)
     member_total = predicted_all.shape[0]
     slot_ids = jnp.arange(OBS_CAP, dtype=jnp.int32)
     valid_slots = (slot_ids < obs_count[0]).astype(jnp.float32)

time: 452 us -> 452 us (level)
  blocking collectives: 13.5 us -> 0 us
  waiting for transfers between devices: 82.1 us -> 89.5 us
    all_gather x1 -> x0, blocking collectives: 13.5 us -> none  [shards(): predicted_all = lax.all_gather(predicted_own, 'ens', axis=0, tiled=True)]
    all_to_all x0 -> x1, waiting for transfers between devices: none -> 7.44 us  [serve_the_rates(): return all_to_all(spare, chip_axis, split_axis=0, concat_axis=0, tiled=True)]
    all_to_all x0 -> x1, starting transfers between devices: none -> 4.71 us  [serve_the_rates(): return all_to_all(spare, chip_axis, split_axis=0, concat_axis=0, tiled=True)]
  transfers between devices with their start and end apart: 6 -> 7, of which waited for: 4 -> 5; matrix products, arithmetic and copies ran while one was open for 46% -> 46% of each run, Pallas kernels for 0% -> 0%
where the time goes in v1:
time: 452 us; the launch traced here: 444 us
  matrix products  144 us (32%)
  other arithmetic  92.2 us (20%)
  waiting for transfers between devices  89.5 us (20%)
  local copies, waits for them, and re-layouts  84.2 us (19%)
  starting transfers between devices  19 us (4%)
  between operations  15.4 us (3%)
    dot_general x16, matrix products, reaction(): jnp.dot(member_coef, hidden_two, preferred_element_type=jnp.float32)  70 us
    all_to_all x1, waiting for transfers between devices, shards(): lax.all_to_all(advected, 'trc', split_axis=2, concat_axis=0, tiled=True)  67.1 us
    dot_general x16, matrix products, reaction(): lax.dot_general(in_weight, fields, contract, preferred_element_type=jnp.f...  66.9 us
    add x2, other arithmetic, transport(): jnp.maximum(north_speed, 0.0) * concentration  30.8 us
    convert_element_type x1, other arithmetic, shards(): transport(tracer_state.astype(jnp.float32) * sea_mask, velocity, sea_mask)  16 us
    sub x1, other arithmetic, transport(): concentration - (east_flux - west_flux) - (north_flux - south_flux)  15.4 us
    ppermute x4, waiting for transfers between devices, tree_sum(): value = value + lax.ppermute(value, axis_name, pairs)  14.9 us
    slice x4, local copies, waits for them, and re-layouts, transport(): east_value = jnp.roll(concentration, -1, axis=-1)  13.4 us
  transfers between devices with their start and end apart: 7, of which 5 were waited for; matrix products, arithmetic and copies ran while one was open for 46% of the time, Pallas kernels for 0%

profile of v1, /device:TPU:6, one launch (start us, length us, event | category | flops | bytes accessed | tf_op | source)
XLA Modules:
  0.0 444.2 jit_solution(7806094792333127996)
XLA Ops:
  8.2 5.3 %convert_multiply_fusion = f32[24,4,16,1440]{3,0,1,2:T(8,128)S(1)} fusion(f32[16,1440]{1,0:T(8,128)S(1)} %convert_element_type.40, bf16[24,4,16,1440]{3,2,1,0:T(8,128)(2,1)} %param.15), kind=kLoop, calls=%fused_computation.34 | loop fusion | flops 4423680 | bytes 13363200 | tf_op jit(solution)/shard_map/mul | solution.py:109
  13.4 6.2 %slice.102 = f32[24,4,16,1439]{3,0,1,2:T(8,128)} slice(f32[24,4,16,1440]{3,0,1,2:T(8,128)S(1)} %convert_multiply_fusion), slice={[0:24], [0:4], [0:16], [1:1440]} | slice | bytes 17682432 | tf_op jit(solution)/shard_map/jit(_roll_static)/slice | solution.py:28
  19.6 4.2 slice.107
  26.2 13.3 %multiply_add_fusion.1 = (f32[24,4,16,1440]{3,0,1,2:T(8,128)S(1)}, f32[24,4,16,1440]{3,0,1,2:T(8,128)S(1)}) fusion(f32[24,4,15,1440]{3,0,1,2:T(8,128)} %slice.107, f32[4,16,1440]{2,0,1:T(4,128)S(1)} %copy.69, f32[4,16,1440]{2,0,1:T(4,128)S(1)} %copy.68, f32[16,1440]{1,0:T(8,128)S(1)} %convert_element_type.40, bf16[24,4,16,1440]{3,2,1,0:T(8,128)(2,1)} %param.15, ...), kind=kLoop, calls=%fused_computation.33 | loop fusion | flops 19906560 | bytes 40826880 | tf_op jit(solution)/shard_map/add | solution.py:36
  39.4 4.8 %slice.108 = f32[24,4,15,1440]{3,0,1,2:T(8,128)} slice(f32[24,4,16,1440]{3,0,1,2:T(8,128)S(1)} %get-tuple-element.101), slice={[0:24], [0:4], [0:15], [0:1440]} | slice | bytes 16588800 | tf_op jit(solution)/shard_map/slice | solution.py:41
  44.2 2.4 slice.104
  46.6 2.1 copy-done.1
  48.8 15.4 %fusion.18 = f32[24,4,16,1440]{3,0,1,2:T(8,128)S(1)} fusion(f32[24,4,16,1440]{3,0,1,2:T(8,128)} %copy-done, f32[24,4,16,1439]{3,0,1,2:T(8,128)} %bitcast.105, f32[24,4,16,1]{3,0,1,2:T(8,128)} %slice.104, f32[24,4,16,1440]{3,0,1,2:T(8,128)} %copy-done.1, f32[24,4,15,1440]{3,0,1,2:T(8,128)} %slice.108, f32[16,1440]{1,0:T(8,128)S(1)} %convert_element_type.40, ...), kind=kLoop, calls=%fused_computation.25 | loop fusion | flops 15482880 | bytes 48199680 | tf_op jit(solution)/shard_map/sub | solution.py:43
  64.1 6.2 %slice.109 = f32[24,4,16,1439]{3,0,1,2:T(8,128)} slice(f32[24,4,16,1440]{3,0,1,2:T(8,128)S(1)} %fusion.18), slice={[0:24], [0:4], [0:16], [1:1440]} | slice | bytes 17682432 | tf_op jit(solution)/shard_map/jit(_roll_static)/slice | solution.py:28
  70.3 4.3 slice.113
  74.7 17.6 %multiply_add_fusion = (f32[24,4,16,1440]{3,0,1,2:T(8,128)}, f32[24,4,16,1440]{3,0,1,2:T(8,128)}) fusion(f32[24,4,15,1440]{3,0,1,2:T(8,128)} %slice.113, f32[24,4,16,1440]{3,0,1,2:T(8,128)S(1)} %fusion.18, f32[4,16,1440]{2,0,1:T(4,128)S(1)} %copy.69, f32[4,16,1440]{2,0,1:T(4,128)S(1)} %copy.68, f32[24,4,16,1]{3,0,1,2:T(8,128)S(1)} %slice.110, ...), kind=kLoop, calls=%fused_computation.32 | loop fusion | flops 15482880 | bytes 45158400 | tf_op jit(solution)/shard_map/add | solution.py:36
  92.3 8.2 %slice.114 = f32[24,4,15,1440]{3,0,1,2:T(8,128)} slice(f32[24,4,16,1440]{3,0,1,2:T(8,128)} %get-tuple-element.99), slice={[0:24], [0:4], [0:15], [0:1440]} | slice | bytes 16588800 | tf_op jit(solution)/shard_map/slice | solution.py:41
  100.6 1.4 slice.111
  102.0 16.0 %fusion.22 = bf16[24,4,16,1440]{3,0,1,2:T(8,128)(2,1)} fusion(f32[24,4,16,1440]{3,0,1,2:T(8,128)S(1)} %fusion.18, f32[24,4,16,1440]{3,0,1,2:T(8,128)} %get-tuple-element.100, f32[24,4,16,1439]{3,0,1,2:T(8,128)} %bitcast.104, f32[24,4,16,1]{3,0,1,2:T(8,128)S(1)} %slice.111, f32[24,4,16,1440]{3,0,1,2:T(8,128)} %get-tuple-element.99, f32[24,4,15,1440]{3,0,1,2:T(8,128)} %slice.114), kind=kLoop, calls=%fused_computation.31 | loop fusion | flops 13271040 | bytes 48107520 | tf_op jit(solution)/shard_map/convert_element_type | solution.py:109
  118.0 8.4 %all-to-all-start = ((bf16[24,4,16,1440]{3,0,1,2:T(8,128)(2,1)}), bf16[24,4,16,1440]{3,0,1,2:T(8,128)(2,1)}, u32[]{:S(2)}, u32[]{:S(2)}) async-start(bf16[24,4,16,1440]{3,0,1,2:T(8,128)(2,1)} %fusion.22), calls=%async_computation | async-start | bytes 9437184 | tf_op jit(solution)/shard_map/all_to_all | solution.py:114
  128.2 67.1 %all-to-all-done = bf16[24,4,16,1440]{3,0,1,2:T(8,128)(2,1)} async-done(((bf16[24,4,16,1440]{3,0,1,2:T(8,128)(2,1)}), bf16[24,4,16,1440]{3,0,1,2:T(8,128)(2,1)}, u32[]{:S(2)}, u32[]{:S(2)}) %all-to-all-start) | async-done | bytes 4423712 | tf_op jit(solution)/shard_map/all_to_all | solution.py:114
  195.3 6.9 %copy.70 = bf16[16,24,4,1,1440]{4,2,1,0,3:T(4,128)(2,1)} copy(bf16[16,24,4,1,1440]{4,1,2,0,3:T(8,128)(2,1)} %bitcast.5) | data formatting | bytes 8847360 | tf_op jit(solution)/shard_map/all_to_all | solution.py:114
  202.3 8.6 %reshape.104 = bf16[16,24,5760]{2,1,0:T(8,128)(2,1)} reshape(bf16[16,24,4,1,1440]{4,2,1,0,3:T(4,128)(2,1)} %copy.70) | data formatting | bytes 8847360 | tf_op jit(solution)/shard_map/reshape | solution.py:116
  210.9 139.0 %while.11 = (s32[]{:T(128)}, bf16[16,24,5760]{2,1,0:T(8,128)(2,1)}, bf16[16,24,5760]{2,1,0:T(8,128)(2,1)}, bf16[16,24,256]{2,1,0:T(8,128)(2,1)S(1)}, bf16[24,256...) while((s32[]{:T(128)}, bf16[16,24,5760]{2,1,0:T(8,128)(2,1)}, ...), condition=%wide.region_1.2_spmd.clone, body=%wide.region_0.1_spmd.clone.sunk | while | flops 914918400 | bytes 6986469 | solution.py:123
  211.0 4.2 multiply_convert_fusion.3
  215.3 4.4 fusion.59
  219.6 4.2 multiply_convert_fusion.3
  224.0 4.4 fusion.59
  228.3 4.2 multiply_convert_fusion.3
  232.6 4.4 fusion.59
  237.0 4.2 multiply_convert_fusion.3
  241.3 4.4 fusion.59
  245.7 4.2 multiply_convert_fusion.3
  250.0 4.4 fusion.59
  254.4 4.2 multiply_convert_fusion.3
  258.7 4.4 fusion.59
  263.1 4.2 multiply_convert_fusion.3
  267.4 4.4 fusion.59
  271.8 4.2 multiply_convert_fusion.3
  276.1 4.4 fusion.59
  280.4 4.2 multiply_convert_fusion.3
  284.8 4.4 fusion.59
  289.1 4.2 multiply_convert_fusion.3
  293.4 4.4 fusion.59
  297.8 4.2 multiply_convert_fusion.3
  302.1 4.4 fusion.59
  306.5 4.2 multiply_convert_fusion.3
  310.8 4.4 fusion.59
  315.2 4.2 multiply_convert_fusion.3
  319.5 4.4 fusion.59
  323.9 4.2 multiply_convert_fusion.3
  328.2 4.4 fusion.59
  332.6 4.2 multiply_convert_fusion.3
  336.9 4.4 fusion.59
  341.3 4.2 multiply_convert_fusion.3
  345.6 4.4 fusion.59
  349.9 1.5 slice.97
  353.7 4.7 %all-to-all-start.1 = ((bf16[128,6,128]{2,1,0:T(8,128)(2,1)}), bf16[128,6,128]{2,1,0:T(8,128)(2,1)S(1)}, u32[]{:S(2)}, u32[]{:S(2)}) async-start(bf16[128,6,128]{2,1,0:T(8,128)(2,1)} %copy.72), calls=%async_computation.1 | async-start | bytes 524288 | tf_op jit(solution)/shard_map/all_to_all | solution.py:19
  358.4 7.4 %all-to-all-done.1 = bf16[128,6,128]{2,1,0:T(8,128)(2,1)S(1)} async-done(((bf16[128,6,128]{2,1,0:T(8,128)(2,1)}), bf16[128,6,128]{2,1,0:T(8,128)(2,1)S(1)}, u32[]{:S(2)}, u32[]{:S(2)}) %all-to-all-start.1) | async-done | bytes 196640 | tf_op jit(solution)/shard_map/all_to_all | solution.py:19
  369.0 5.0 %collective-permute-done = f32[2,128,128]{2,1,0:T(8,128)S(1)} collective-permute-done((f32[2,128,128]{2,1,0:T(8,128)S(1)}, f32[2,128,128]{2,1,0:T(8,128)S(1)}, u32[]{:S(2)}, u32[]{:S(2)}) %collective-permute-start) | collective-permute-done | bytes 131104 | tf_op jit(solution)/shard_map/ppermute | solution.py:57
  373.9 1.7 collective-permute-start.1
  375.7 4.8 %collective-permute-done.1 = f32[2,128,128]{2,1,0:T(8,128)S(1)} collective-permute-done((f32[2,128,128]{2,1,0:T(8,128)S(1)}, f32[2,128,128]{2,1,0:T(8,128)S(1)}, u32[]{:S(2)}, u32[]{:S(2)}) %collective-permute-start.1) | collective-permute-done | bytes 131104 | tf_op jit(solution)/shard_map/ppermute | solution.py:57
  381.0 5.1 %collective-permute-done.2 = f32[2,128,128]{2,1,0:T(8,128)S(1)} collective-permute-done((f32[2,128,128]{2,1,0:T(8,128)S(1)}, f32[2,128,128]{2,1,0:T(8,128)S(1)}, u32[]{:S(2)}, u32[]{:S(2)}) %collective-permute-start.2) | collective-permute-done | bytes 131104 | tf_op jit(solution)/shard_map/ppermute | solution.py:57
  386.2 3.6 collective-permute-start.3
  389.7 10.5 %reshape.105 = bf16[384,4,1,1440]{3,1,0,2:T(4,128)(2,1)} reshape(bf16[16,24,5760]{2,1,0:T(8,128)(2,1)} %get-tuple-element.49) | data formatting | bytes 8847360 | tf_op jit(solution)/shard_map/reshape | solution.py:124
  400.2 8.8 %copy.80 = bf16[384,4,1,1440]{0,3,2,1:T(8,128)(2,1)} copy(bf16[384,4,1,1440]{3,1,0,2:T(4,128)(2,1)} %reshape.105) | data formatting | bytes 8847360
  409.2 11.7 %cholesky.16 = f32[128,128]{1,0:T(8,128)S(1)} custom-call(f32[128,128]{1,0:T(8,128)S(1)} %fusion.35), custom_call_target="Cholesky" | custom-call | tf_op jit(solution)/shard_map/jit(cholesky)/cholesky | solution.py:77
  422.3 9.8 %custom-call.8 = f32[1,128,128]{1,2,0:T(8,128)S(1)} custom-call(f32[1,128,128]{2,1,0:T(8,128)S(1)} %fusion.29), custom_call_target="InvertDiagBlocksLowerTriangular" | custom-call | tf_op jit(solution)/shard_map/triangular_solve | solution.py:79
  432.8 3.5 convolution_add_fusion.2
  (113 shorter events, 15.2 us)
Async XLA Ops:
  19.6 5.2 %copy-start.6 = (s32[16,1440]{1,0:T(8,128)S(1)}, s32[16,1440]{1,0:T(8,128)}, u32[]{:S(2)}) copy-start(s32[16,1440]{1,0:T(8,128)} %param.17) | copy-start | bytes 276484
  19.6 5.3 %copy-start.4 = (f32[2,4,16,1440]{3,2,1,0:T(8,128)S(1)}, f32[2,4,16,1440]{3,2,1,0:T(8,128)}, u32[]{:S(2)}) copy-start(f32[2,4,16,1440]{3,2,1,0:T(8,128)} %param.16) | copy-start | bytes 2211844
  39.4 7.2 %copy-start = (f32[24,4,16,1440]{3,0,1,2:T(8,128)}, f32[24,4,16,1440]{3,0,1,2:T(8,128)S(1)}, u32[]{:S(2)}) copy-start(f32[24,4,16,1440]{3,0,1,2:T(8,128)S(1)} %get-tuple-element.102) | copy-start | bytes 26542084
  39.4 9.3 %copy-start.1 = (f32[24,4,16,1440]{3,0,1,2:T(8,128)}, f32[24,4,16,1440]{3,0,1,2:T(8,128)S(1)}, u32[]{:S(2)}) copy-start(f32[24,4,16,1440]{3,0,1,2:T(8,128)S(1)} %get-tuple-element.101) | copy-start | bytes 26542084
  118.0 8.5 %copy-start.3 = (f32[16,24,256]{2,1,0:T(8,128)S(1)}, f32[16,24,256]{2,1,0:T(8,128)}, u32[]{:S(2)}) copy-start(f32[16,24,256]{2,1,0:T(8,128)} %param.22) | copy-start | bytes 1179652
  118.0 10.2 %copy-start.7 = (f32[1,6,128]{2,0,1:T(1,128)S(1)}, f32[1,6,128]{2,0,1:T(1,128)}, u32[]{:S(2)}) copy-start(f32[1,6,128]{2,0,1:T(1,128)} %param.25) | copy-start | bytes 9220
  118.0 77.3 %all-to-all-start = ((bf16[24,4,16,1440]{3,0,1,2:T(8,128)(2,1)}), bf16[24,4,16,1440]{3,0,1,2:T(8,128)(2,1)}, u32[]{:S(2)}, u32[]{:S(2)}) async-start(bf16[24,4,16,1440]{3,0,1,2:T(8,128)(2,1)} %fusion.22), calls=%async_computation | async-start | bytes 9437184 | tf_op jit(solution)/shard_map/all_to_all | solution.py:114
  126.4 306.4 %all-gather.2.cloned.1.call-start = ((), (), s32[]{:S(2)}) async-start(), calls=%async_computation.2 | async-start | bytes 3538944 | tf_op jit(solution)/shard_map/all_gather | solution.py:108
  127.4 83.5 %copy-start.9 = (bf16[256,256]{1,0:T(8,128)(2,1)S(1)}, bf16[256,256]{1,0:T(8,128)(2,1)}, u32[]{:S(2)}) copy-start(bf16[256,256]{1,0:T(8,128)(2,1)} %param.20) | copy-start | bytes 393220
  127.4 83.5 %copy-start.10 = (bf16[24,256]{1,0:T(8,128)(2,1)S(1)}, bf16[24,256]{1,0:T(8,128)(2,1)}, u32[]{:S(2)}) copy-start(bf16[24,256]{1,0:T(8,128)(2,1)} %param.18) | copy-start | bytes 36868
  127.4 83.5 %copy-start.11 = (f32[256]{0:T(256)S(1)}, f32[256]{0:T(256)}, u32[]{:S(2)}) copy-start(f32[256]{0:T(256)} %param.19) | copy-start | bytes 3076
  127.4 83.5 %copy-start.12 = (f32[256]{0:T(256)S(1)}, f32[256]{0:T(256)}, u32[]{:S(2)}) copy-start(f32[256]{0:T(256)} %param.21) | copy-start | bytes 3076
  210.9 141.0 %copy-start.13 = (s32[1,128]{1,0:T(1,128)S(1)}, s32[1,128]{1,0:T(1,128)}, u32[]{:S(2)}) copy-start(s32[1,128]{1,0:T(1,128)} %param.23) | copy-start | bytes 1540
  210.9 147.4 %copy-start.8 = (f32[1,6,128]{2,0,1:T(1,128)S(1)}, f32[1,6,128]{2,0,1:T(1,128)}, u32[]{:S(2)}) copy-start(f32[1,6,128]{2,0,1:T(1,128)} %param.26) | copy-start | bytes 9220
  349.9 16.3 %copy-start.5 = (f32[128,1,6,128]{3,1,2,0:T(1,128)S(1)}, f32[128,1,6,128]{3,1,2,0:T(1,128)}, u32[]{:S(2)}) copy-start(f32[128,1,6,128]{3,1,2,0:T(1,128)} %param.27) | copy-start | bytes 1179652
  353.7 12.2 %all-to-all-start.1 = ((bf16[128,6,128]{2,1,0:T(8,128)(2,1)}), bf16[128,6,128]{2,1,0:T(8,128)(2,1)S(1)}, u32[]{:S(2)}, u32[]{:S(2)}) async-start(bf16[128,6,128]{2,1,0:T(8,128)(2,1)} %copy.72), calls=%async_computation.1 | async-start | bytes 524288 | tf_op jit(solution)/shard_map/all_to_all | solution.py:19
  368.9 5.0 %collective-permute-start = (f32[2,128,128]{2,1,0:T(8,128)S(1)}, f32[2,128,128]{2,1,0:T(8,128)S(1)}, u32[]{:S(2)}, u32[]{:S(2)}) collective-permute-start(f32[2,128,128]{2,1,0:T(8,128)S(1)} %pad_maximum_fusion), channel_id=1, source_target_pairs={{0,1},{1,0},{2,3},{3,2},{4,5},{5,4},{6,7},{7,6},{8,9},{9,8},{10,11... | collective-permute-start | bytes 393224 | tf_op jit(solution)/shard_map/ppermute | solution.py:57
  373.9 6.6 %collective-permute-start.1 = (f32[2,128,128]{2,1,0:T(8,128)S(1)}, f32[2,128,128]{2,1,0:T(8,128)S(1)}, u32[]{:S(2)}, u32[]{:S(2)}) collective-permute-start(f32[2,128,128]{2,1,0:T(8,128)S(1)} %fusion.38), channel_id=1, source_target_pairs={{0,2},{1,3},{2,0},{3,1},{4,6},{5,7},{6,4},{7,5},{8,10},{9,11},{10,... | collective-permute-start | bytes 393224 | tf_op jit(solution)/shard_map/ppermute | solution.py:57
  380.5 5.6 %collective-permute-start.2 = (f32[2,128,128]{2,1,0:T(8,128)S(1)}, f32[2,128,128]{2,1,0:T(8,128)S(1)}, u32[]{:S(2)}, u32[]{:S(2)}) collective-permute-start(f32[2,128,128]{2,1,0:T(8,128)S(1)} %fusion.47), channel_id=1, source_target_pairs={{0,4},{1,5},{2,6},{3,7},{4,0},{5,1},{6,2},{7,3},{8,12},{9,13},{10,... | collective-permute-start | bytes 393224 | tf_op jit(solution)/shard_map/ppermute | solution.py:57
  386.2 22.9 %collective-permute-start.3 = (f32[2,128,128]{2,1,0:T(8,128)S(1)}, f32[2,128,128]{2,1,0:T(8,128)S(1)}, u32[]{:S(2)}, u32[]{:S(2)}) collective-permute-start(f32[2,128,128]{2,1,0:T(8,128)S(1)} %add.113), channel_id=1, source_target_pairs={{0,8},{1,9},{2,10},{3,11},{4,12},{5,13},{6,14},{7,15},{8,0},{9,1},... | collective-permute-start | bytes 393224 | tf_op jit(solution)/shard_map/ppermute | solution.py:57
  389.7 43.0 %copy-start.2 = (f32[2,8,24,256]{3,1,2,0:T(8,128)S(1)}, f32[2,8,24,256]{3,1,2,0:T(8,128)}, u32[]{:S(2)}) copy-start(f32[2,8,24,256]{3,1,2,0:T(8,128)} %copy.85) | copy-start | bytes 1179652
Sparse Core Ops, SparseCore 0:
  129.5 28.9 all-gather.1
